TPU v7x, 256 devices: a whole 4x4x8 slice. The times are simulated.
256 devices in a mesh: dp: 32 (over x, z), segment: 2 (over core), rows: 4 (over y).
Axes of the slice: x: 4, y: 4, z: 8, core: 2. Of those that a mesh axis runs over, the one named last changes fastest.
Arguments:
- block_input: bfloat16 [32, 16, 32, 416], P('dp', 'rows'), may hold values from -6 to 6
- saved_maps: bfloat16 [2, 32, 16, 32, 2496], P('segment', 'dp', 'rows'), may hold values from -6 to 6
- grad_p5: bfloat16 [32, 16, 32, 384], P('dp', 'rows'), may hold values from -6 to 6
- grad_p6: bfloat16 [32, 8, 16, 384], P('dp', 'rows'), may hold values from -12 to 12
- grad_p7: bfloat16 [32, 4, 8, 384], P('dp', 'rows'), may hold values from -16 to 16
- lateral: bfloat16 [416, 384], replicated, may hold values from -0.3125 to 0.3125
- stacked: bfloat16 [2, 1038336], P('segment', ('dp', 'rows')), may hold values from -0.3125 to 0.3125
- kernel: bfloat16 [25, 2496], replicated, may hold values from -1.75 to 1.75
- se_reduce: bfloat16 [2496, 104], replicated, may hold values from -0.3125 to 0.3125
- se_expand: bfloat16 [104, 2496], replicated, may hold values from -1.25 to 1.25
Outputs:
- grad_inputs: bfloat16 [2, 32, 16, 32, 416], P('segment', 'dp', 'rows')
- param_grads: float32 [2, 1038336], P('segment', ('dp', 'rows'))
All inputs are finite; a program needn't handle non-finite values.
Results may differ from a plain program's by a relative error of at most 0.0059.
Values may be sent and summed in bfloat16 or wider, within the bound.
No kernel may reach another device: no remote copies, remote signals or barrier semaphores. Data moves between devices by JAX's collectives and lax.ppermute only.
A program may use at most 64 MiB of HBM per device.

v0:
```python
import jax
import jax.numpy as jnp
from jax import lax
from jax.sharding import PartitionSpec as P


def extended_2(block, sides, width):
    for axis, dim in sides:
        count = lax.axis_size(axis)
        forward = [(i, i + 1) for i in range(count - 1)]
        backward = [(target, source) for source, target in forward]
        low = lax.ppermute(
            lax.slice_in_dim(block, block.shape[dim] - width, None, axis=dim), axis, forward
        )
        high = lax.ppermute(lax.slice_in_dim(block, 0, width, axis=dim), axis, backward)
        block = jnp.concatenate([low, block, high], axis=dim)
    return block


def passed_along(array, axis, by):
    length = lax.axis_size(axis)
    pairs = [(i, i + by) for i in range(length) if 0 <= i + by < length]
    return lax.ppermute(array, axis, pairs)


def up_two(v):
    return jnp.repeat(jnp.repeat(v, 2, axis=0), 2, axis=1)


def silu_slope(v):
    sig = jax.nn.sigmoid(v)
    return sig * (1.0 + v * (1.0 - sig))


def depth_forward(padded, taps, rows, cols):
    total = jnp.zeros((rows, cols, taps.shape[1]), jnp.float32)
    for p in range(5):
        for q in range(5):
            total = total + taps[5 * p + q] * padded[p : p + rows, q : q + cols].astype(jnp.float32)
    return total


def depth_backward(padded, taps, rows, cols):
    total = jnp.zeros((rows, cols, taps.shape[1]), jnp.float32)
    for p in range(5):
        for q in range(5):
            total = total + taps[5 * p + q] * padded[
                4 - p : 4 - p + rows, 4 - q : 4 - q + cols
            ].astype(jnp.float32)
    return total


def margin(values):
    extended = extended_2(values, (("rows", 0),), 2)
    return jnp.pad(extended, ((0, 0), (2, 2), (0, 0)))


def squeeze_gate(pool_total, grad_total, cells, reduce_w, expand_w):
    pooled = pool_total / cells
    z1 = jnp.dot(pooled, reduce_w, precision=lax.Precision.HIGHEST)
    z2 = jnp.dot(jax.nn.silu(z1), expand_w, precision=lax.Precision.HIGHEST)
    gate = jax.nn.sigmoid(z2)
    dz2 = grad_total * gate * (1.0 - gate)
    dz1 = jnp.dot(dz2, expand_w.T, precision=lax.Precision.HIGHEST) * silu_slope(z1)
    dpool = jnp.dot(dz1, reduce_w.T, precision=lax.Precision.HIGHEST)
    return (gate, dpool)


def body(
    block_input,
    saved_maps,
    grad_p5,
    grad_p6,
    grad_p7,
    lateral,
    stacked,
    kernel,
    se_reduce,
    se_expand,
):
    rows_here = block_input.shape[1]
    cols = block_input.shape[2]
    cin = block_input.shape[3]
    wide = saved_maps.shape[-1]
    cells_here = rows_here * cols
    row_count = lax.axis_size("rows")
    cells = cells_here * row_count
    images = block_input.shape[0] * lax.axis_size("dp")
    flat = lax.all_gather(stacked[0], ("dp", "rows"), axis=0, tiled=True)
    weight = flat.reshape(cin, wide)
    segment = lax.axis_index("segment")
    held = saved_maps[0, 0]
    image = block_input[0]
    taps = kernel.astype(jnp.float32)
    reduce_w = se_reduce.astype(jnp.float32)
    expand_w = se_expand.astype(jnp.float32)

    def head_branch():
        inner = grad_p6[0].astype(jnp.float32) + up_two(grad_p7[0].astype(jnp.float32)) / 4.0
        g = (grad_p5[0].astype(jnp.float32) + up_two(inner) / 4.0).astype(jnp.bfloat16)
        grad_out = jnp.dot(
            g.reshape(cells_here, -1), lateral.T, preferred_element_type=jnp.float32
        ).astype(jnp.bfloat16)
        grad_proj = jnp.dot(grad_out, weight, preferred_element_type=jnp.float32).astype(
            jnp.bfloat16
        )
        term = jnp.dot(
            grad_out.T, held.reshape(cells_here, wide), preferred_element_type=jnp.float32
        )
        return (
            grad_out.reshape(rows_here, cols, cin),
            grad_proj.reshape(rows_here, cols, wide),
            term,
        )

    def rise_branch():
        expanded = jax.nn.silu(held.astype(jnp.float32)).astype(jnp.bfloat16)
        return (
            jnp.zeros((rows_here, cols, cin), jnp.bfloat16),
            expanded,
            jnp.zeros((cin, wide), jnp.float32),
        )

    grad_top, middle, head_term = lax.cond(segment == 0, head_branch, rise_branch)
    sent_top, sent_mid = passed_along((grad_top, middle), "segment", 1)
    padded_e = margin(middle)

    def pool_branch():
        dwo = depth_forward(padded_e, taps, rows_here, cols)
        act = jax.nn.silu(dwo)
        pool_part = jnp.sum(act, axis=(0, 1))
        grad_part = jnp.sum(sent_mid.astype(jnp.float32) * act, axis=(0, 1))
        return (dwo, pool_part, grad_part)

    def still_branch():
        return (
            jnp.zeros((rows_here, cols, wide), jnp.float32),
            jnp.zeros((wide,), jnp.float32),
            jnp.zeros((wide,), jnp.float32),
        )

    dwo, pool_part, grad_part = lax.cond(segment == 1, pool_branch, still_branch)
    pool_total, grad_total = lax.psum((pool_part, grad_part), "rows")

    def gate_branch():
        gate, dpool = squeeze_gate(pool_total, grad_total, cells, reduce_w, expand_w)
        return ((sent_mid.astype(jnp.float32) * gate + dpool / cells) * silu_slope(dwo)).astype(
            jnp.bfloat16
        )

    def quiet_branch():
        return jnp.zeros((rows_here, cols, wide), jnp.bfloat16)

    grad_dw = lax.cond(segment == 1, gate_branch, quiet_branch)
    padded_grad = margin(grad_dw)

    def tail_branch():
        grad_e = depth_backward(padded_grad, taps, rows_here, cols)
        grad_pre = (
            (grad_e * silu_slope(held.astype(jnp.float32)))
            .astype(jnp.bfloat16)
            .reshape(cells_here, wide)
        )
        term = jnp.dot(
            image.reshape(cells_here, cin).T, grad_pre, preferred_element_type=jnp.float32
        )
        back = jnp.dot(grad_pre, weight.T, preferred_element_type=jnp.float32)
        grad_x = (sent_top.reshape(cells_here, cin).astype(jnp.float32) + back).astype(jnp.bfloat16)
        return (grad_x.reshape(rows_here, cols, cin), term)

    def head_keep():
        return (grad_top, head_term)

    grad_here, term = lax.cond(segment == 1, tail_branch, head_keep)
    flat_term = (term / images).reshape(-1)
    share = lax.psum_scatter(flat_term, ("dp", "rows"), scatter_dimension=0, tiled=True)
    return (grad_here[None, None], share[None])


def solution(mesh):
    in_specs = (
        P("dp", "rows", None, None),
        P("segment", "dp", "rows", None, None),
        P("dp", "rows", None, None),
        P("dp", "rows", None, None),
        P("dp", "rows", None, None),
        P(),
        P("segment", ("dp", "rows")),
        P(),
        P(),
        P(),
    )
    out_specs = (P("segment", "dp", "rows", None, None), P("segment", ("dp", "rows")))
    return jax.shard_map(body, mesh=mesh, in_specs=in_specs, out_specs=out_specs, check_vma=False)
```

profile of v0, /device:TPU:8, one launch (start us, length us, event | category | flops | bytes accessed | tf_op | source)
XLA Modules:
  0.0 562.4 jit_solution(10256133657694480571)
XLA Ops:
  7.2 0.0 all-reduce.8.cloned.1.call-start
  7.2 1.4 fusion.28
  9.3 0.9 reduce.52
  10.2 0.1 broadcast.72
  10.3 0.4 dynamic-update-slice
  10.7 1.3 copy-done.1
  12.0 0.0 all-reduce.8.cloned.1.call-update
  12.0 0.0 all-reduce.10.cloned.1.call-start
  12.1 0.0 copy-start.2
  12.1 0.0 copy-start.8
  12.1 0.0 copy-start.11
  12.2 230.4 %all-reduce.8.cloned.1.call-done = bf16[1038336]{0:T(1024)(128)(2,1)} async-done(((bf16[1038336]{0:T(1024)(128)(2,1)}), bf16[1038336]{0:T(1024)(128)(2,1)}) %all-reduce.8.cloned.1.call-update) | async-done | bytes 2076688
  242.6 3.5 reshape.102
  246.1 7.1 %conditional.4 = (bf16[4,32,416]{2,1,0:T(8,128)(2,1)}, bf16[4,32,2496]{2,1,0:T(8,128)(2,1)}, f32[416,2496]{1,0:T(8,128)}) conditional(s32[]{:T(128)} %convert_element_type.231, bf16[4,32,2496]{2,1,0:T(8,128)(2,1)S(1)} %bitcast.59, (bf16[1,4,32,384]{3,2,1,0:T(8,128)(2,1)}, bf16[1,2,16,384]{3,2,1,0:T(8,128)(2,1)S(1)}, ...), branch_computations={%region_0.1_spmd, %region_1.2_spmd} | conditional | flops 573085696 | bytes 10971160 | solution.py:124
  246.2 0.1 broadcast_in_dim.20
  246.3 0.1 div.37
  246.4 1.2 convolution_convert_fusion.1
  247.6 2.7 fusion.29
  250.2 1.1 convolution_convert_fusion
  251.4 1.1 copy.30
  252.4 0.8 copy.29
  253.2 2.0 fusion.27
  255.2 3.4 collective-permute-start.1
  258.6 3.2 collective-permute-start.2
  261.8 2.2 collective-permute-start
  264.0 0.8 convert_element_type.232
  264.7 1.1 copy.33
  265.8 1.2 convert_element_type.233
  267.1 0.0 copy-done.7
  267.1 1.1 convert_element_type.234
  268.2 1.5 pad_maximum_fusion
  269.7 1.2 conditional.5
  269.7 1.2 broadcast.61
  270.9 13.9 %all-reduce.4 = (f32[2496]{0:T(1024)S(1)}, f32[2496]{0:T(1024)S(1)}) all-reduce(f32[2496]{0:T(1024)S(1)} %get-tuple-element.93, f32[2496]{0:T(1024)S(1)} %get-tuple-element.94), channel_id=1, replica_groups=mesh['dp'=32,'segment'=2,'rows'=4] {'rows'}, use_global_device_ids=true, to_apply=%region_6.7 | all-reduce | flops 4992 | bytes 39936 | tf_op jit(solution)/shard_map/psum | solution.py:143
  284.8 0.2 conditional.6
  285.1 4.7 collective-permute-start.3
  289.9 1.9 collective-permute-start.4
  291.8 6.3 %collective-permute-start.5 = (bf16[4,32,416]{2,1,0:T(8,128)(2,1)}, bf16[4,32,416]{2,1,0:T(8,128)(2,1)S(1)}, u32[]{:S(2)}, u32[]{:S(2)}) collective-permute-start(bf16[4,32,416]{2,1,0:T(8,128)(2,1)} %get-tuple-element.189), channel_id=1, source_target_pairs={{0,4},{1,5},{2,6},{3,7},{8,12},{9,13},{10,14},{11,15},{16,20},{17,... | collective-permute-start | bytes 319496 | tf_op jit(solution)/shard_map/ppermute | solution.py:23
  298.1 0.0 copy-start.3
  298.1 0.7 collective-permute-done.4
  298.9 0.2 pad_maximum_fusion.1
  299.0 0.3 collective-permute-done.5
  299.3 0.0 copy-done.10
  299.3 4.5 broadcast_multiply_fusion.2
  303.8 5.8 %reshape.103 = f32[1038336]{0:T(1024)} reshape(f32[416,2496]{1,0:T(8,128)} %broadcast_multiply_fusion.2) | data formatting | bytes 8306688 | tf_op jit(solution)/shard_map/reshape | solution.py:175
  309.6 0.0 all-reduce.10.cloned.1.call-update
  310.3 243.8 %all-reduce.10.cloned.1.call-done = f32[1038336]{0:T(1024)} async-done(((f32[1038336]{0:T(1024)}), f32[1038336]{0:T(1024)}) %all-reduce.10.cloned.1.call-update) | async-done | bytes 4153360
  554.1 1.5 dynamic-slice.2
  (31 shorter events, 0.2 us)
Async XLA Ops:
  7.2 235.4 %all-reduce.8.cloned.1.call-start = ((), (), s32[]{:S(2)}) async-start(), calls=%async_computation | async-start | bytes 4153344
  10.7 1.3 copy-start.1
  12.0 542.0 %all-reduce.10.cloned.1.call-start = ((), (), s32[]{:S(2)}) async-start(), calls=%async_computation.1 | async-start | bytes 8306688
  12.1 233.9 %copy-start.2 = (bf16[1,1,4,32,2496]{4,3,2,1,0:T(8,128)(2,1)S(1)}, bf16[1,1,4,32,2496]{4,3,2,1,0:T(8,128)(2,1)}, u32[]{:S(2)}) copy-start(bf16[1,1,4,32,2496]{4,3,2,1,0:T(8,128)(2,1)} %param.19) | copy-start | bytes 1916932
  12.1 233.9 %copy-start.8 = (bf16[416,384]{1,0:T(8,128)(2,1)S(1)}, bf16[416,384]{1,0:T(8,128)(2,1)}, u32[]{:S(2)}) copy-start(bf16[416,384]{1,0:T(8,128)(2,1)} %param.23) | copy-start | bytes 958468
  12.1 233.9 %copy-start.11 = (bf16[1,2,16,384]{3,2,1,0:T(8,128)(2,1)S(1)}, bf16[1,2,16,384]{3,2,1,0:T(8,128)(2,1)}, u32[]{:S(2)}) copy-start(bf16[1,2,16,384]{3,2,1,0:T(8,128)(2,1)} %param.21) | copy-start | bytes 73732
  12.1 233.9 %copy-start.12 = (bf16[1,1,8,384]{3,2,1,0:T(8,128)(2,1)S(1)}, bf16[1,1,8,384]{3,2,1,0:T(8,128)(2,1)}, u32[]{:S(2)}) copy-start(bf16[1,1,8,384]{3,2,1,0:T(8,128)(2,1)} %param.22) | copy-start | bytes 18436
  253.2 10.7 %copy-start.9 = (bf16[25,2496]{1,0:T(8,128)(2,1)S(1)}, bf16[25,2496]{1,0:T(8,128)(2,1)}, u32[]{:S(2)}) copy-start(bf16[25,2496]{1,0:T(8,128)(2,1)} %param.25) | copy-start | bytes 374404
  253.2 11.5 %copy-start.6 = (bf16[2496,104]{0,1:T(8,128)(2,1)S(1)}, bf16[2496,104]{0,1:T(8,128)(2,1)}, u32[]{:S(2)}) copy-start(bf16[2496,104]{0,1:T(8,128)(2,1)} %param.26) | copy-start | bytes 1557508
  255.2 12.9 %collective-permute-start.1 = (bf16[2,32,2496]{2,1,0:T(8,128)(2,1)}, bf16[2,32,2496]{2,1,0:T(8,128)(2,1)}, u32[]{:S(2)}, u32[]{:S(2)}) collective-permute-start(bf16[2,32,2496]{2,1,0:T(8,128)(2,1)} %get-tuple-element.169), channel_id=1, source_target_pairs={{0,1},{1,2},{2,3},{4,5},{5,6},{6,7},{8,9},{9,10},{10,11},{12,13},{... | collective-permute-start | bytes 958472 | tf_op jit(solution)/shard_map/ppermute | solution.py:12
  258.6 9.6 %collective-permute-start.2 = (bf16[2,32,2496]{2,1,0:T(8,128)(2,1)}, bf16[2,32,2496]{2,1,0:T(8,128)(2,1)}, u32[]{:S(2)}, u32[]{:S(2)}) collective-permute-start(bf16[2,32,2496]{2,1,0:T(8,128)(2,1)} %get-tuple-element.170), channel_id=1, source_target_pairs={{1,0},{2,1},{3,2},{5,4},{6,5},{7,6},{9,8},{10,9},{11,10},{13,12},{... | collective-permute-start | bytes 958472 | tf_op jit(solution)/shard_map/ppermute | solution.py:15
  261.8 7.9 %collective-permute-start = (bf16[4,32,2496]{2,1,0:T(8,128)(2,1)}, bf16[4,32,2496]{2,1,0:T(8,128)(2,1)}, u32[]{:S(2)}, u32[]{:S(2)}) collective-permute-start(bf16[4,32,2496]{2,1,0:T(8,128)(2,1)} %get-tuple-element.92), channel_id=1, source_target_pairs={{0,4},{1,5},{2,6},{3,7},{8,12},{9,13},{10,14},{11,15},{16,20},{17,... | collective-permute-start | bytes 1916936 | tf_op jit(solution)/shard_map/ppermute | solution.py:23
  265.8 1.2 copy-start.7
  268.2 1.5 copy-start.4
  285.1 13.0 %collective-permute-start.3 = (bf16[2,32,2496]{2,1,0:T(8,128)(2,1)S(1)}, bf16[2,32,2496]{2,1,0:T(8,128)(2,1)S(1)}, u32[]{:S(2)}, u32[]{:S(2)}) collective-permute-start(bf16[2,32,2496]{2,1,0:T(8,128)(2,1)S(1)} %get-tuple-element.167), channel_id=1, source_target_pairs={{0,1},{1,2},{2,3},{4,5},{5,6},{6,7},{8,9},{9,10},{10,11},{12,13},{... | collective-permute-start | bytes 958472 | tf_op jit(solution)/shard_map/ppermute | solution.py:12
  289.9 9.0 %collective-permute-start.4 = (bf16[2,32,2496]{2,1,0:T(8,128)(2,1)S(1)}, bf16[2,32,2496]{2,1,0:T(8,128)(2,1)S(1)}, u32[]{:S(2)}, u32[]{:S(2)}) collective-permute-start(bf16[2,32,2496]{2,1,0:T(8,128)(2,1)S(1)} %get-tuple-element.168), channel_id=1, source_target_pairs={{1,0},{2,1},{3,2},{5,4},{6,5},{7,6},{9,8},{10,9},{11,10},{13,12},{... | collective-permute-start | bytes 958472 | tf_op jit(solution)/shard_map/ppermute | solution.py:15
  291.8 7.5 %collective-permute-start.5 = (bf16[4,32,416]{2,1,0:T(8,128)(2,1)}, bf16[4,32,416]{2,1,0:T(8,128)(2,1)S(1)}, u32[]{:S(2)}, u32[]{:S(2)}) collective-permute-start(bf16[4,32,416]{2,1,0:T(8,128)(2,1)} %get-tuple-element.189), channel_id=1, source_target_pairs={{0,4},{1,5},{2,6},{3,7},{8,12},{9,13},{10,14},{11,15},{16,20},{17,... | collective-permute-start | bytes 319496 | tf_op jit(solution)/shard_map/ppermute | solution.py:23
  298.1 1.2 copy-start.3
  298.1 1.2 copy-start.5
  298.1 1.2 copy-start.10
Sparse Core Ops, SparseCore 0:
  13.4 229.0 all-reduce.7
  309.7 244.3 all-reduce.9
where the time goes:
time: 563 us; the launch traced here: 562 us
  waiting for transfers between devices  475 us (84%)
  starting transfers between devices  21.7 us (4%)
  local copies, waits for them, and re-layouts  20.6 us (4%)
  between operations  15.6 us (3%)
  blocking collectives  13.9 us (2%)
  other arithmetic  10.1 us (2%)
    unnamed x4, waiting for transfers between devices  474 us
    psum x1, blocking collectives, body(): pool_total, grad_total = lax.psum((pool_part, grad_part), 'rows')  13.9 us
  transfers between devices with their start and end apart: 8, of which 4 were waited for; matrix products, arithmetic and copies ran while one was open for 1% of the time, Pallas kernels for 0%

commit v1 on v0

--- a/solution.py
+++ b/solution.py
@@ -21,6 +21,55 @@
     length = lax.axis_size(axis)
     pairs = [(i, i + by) for i in range(length) if 0 <= i + by < length]
     return lax.ppermute(array, axis, pairs)
+
+
+def flat_bits():
+    rows_bits = lax.axis_size("rows").bit_length() - 1
+    dp_bits = lax.axis_size("dp").bit_length() - 1
+    return [("rows", k) for k in range(rows_bits)] + [("dp", k) for k in range(dp_bits)]
+
+
+def swap_pairs(axis, j):
+    return [(i, i ^ (1 << j)) for i in range(lax.axis_size(axis))]
+
+
+def gather_chunks(piece, order):
+    bits = flat_bits()
+    buf = piece
+    lead = []
+    for axis, j in order:
+        recv = lax.ppermute(buf, axis, swap_pairs(axis, j))
+        high = (lax.axis_index(axis) >> j) & 1
+        buf = jnp.stack([jnp.where(high == 0, buf, recv), jnp.where(high == 0, recv, buf)])
+        lead.insert(0, bits.index((axis, j)))
+    count = len(bits)
+    perm = [lead.index(k) for k in reversed(range(count))] + [count, count + 1]
+    return jnp.transpose(buf, perm).reshape(-1)
+
+
+def scatter_chunks(full, order):
+    bits = flat_bits()
+    count = len(bits)
+    buf = full.reshape((2,) * count + full.shape[1:])
+    live = list(reversed(range(count)))
+    for axis, j in order:
+        at = live.index(bits.index((axis, j)))
+        high = (lax.axis_index(axis) >> j) & 1
+        mine = lax.dynamic_index_in_dim(buf, high, at, keepdims=False)
+        other = lax.dynamic_index_in_dim(buf, 1 - high, at, keepdims=False)
+        buf = mine + lax.ppermute(other, axis, swap_pairs(axis, j))
+        live.pop(at)
+    return buf.reshape(-1)
+
+
+def rows_sum(values):
+    for j in range(lax.axis_size("rows").bit_length() - 1):
+        values = tuple(v + lax.ppermute(v, "rows", swap_pairs("rows", j)) for v in values)
+    return values
+
+
+GATHER_ORDER = [("dp", 2), ("dp", 4), ("dp", 1), ("rows", 1), ("dp", 3), ("dp", 0), ("rows", 0)]
+SCATTER_ORDER = GATHER_ORDER[::-1]
 
 
 def up_two(v):
@@ -86,7 +135,7 @@
     row_count = lax.axis_size("rows")
     cells = cells_here * row_count
     images = block_input.shape[0] * lax.axis_size("dp")
-    flat = lax.all_gather(stacked[0], ("dp", "rows"), axis=0, tiled=True)
+    flat = gather_chunks(stacked[0].reshape(16, -1), GATHER_ORDER)
     weight = flat.reshape(cin, wide)
     segment = lax.axis_index("segment")
     held = saved_maps[0, 0]
@@ -140,7 +189,7 @@
         )
 
     dwo, pool_part, grad_part = lax.cond(segment == 1, pool_branch, still_branch)
-    pool_total, grad_total = lax.psum((pool_part, grad_part), "rows")
+    pool_total, grad_total = rows_sum((pool_part, grad_part))
 
     def gate_branch():
         gate, dpool = squeeze_gate(pool_total, grad_total, cells, reduce_w, expand_w)
@@ -172,8 +221,9 @@
         return (grad_top, head_term)
 
     grad_here, term = lax.cond(segment == 1, tail_branch, head_keep)
-    flat_term = (term / images).reshape(-1)
-    share = lax.psum_scatter(flat_term, ("dp", "rows"), scatter_dimension=0, tiled=True)
+    shards = lax.axis_size("dp") * row_count
+    flat_term = (term / images).reshape(shards, 8, -1)
+    share = scatter_chunks(flat_term, SCATTER_ORDER)
     return (grad_here[None, None], share[None])
 
 

time: 563 us -> 241 us (0.43)
  the two profiles are of different devices: /device:TPU:8 before, /device:TPU:1 now
where the time goes in v1:
time: 241 us; the launch traced here: 240 us
  waiting for transfers between devices  122 us (51%)
  starting transfers between devices  50.3 us (21%)
  other arithmetic  30.6 us (13%)
  local copies, waits for them, and re-layouts  28.6 us (12%)
  matrix products  7.06 us (3%)
    ppermute x7, waiting for transfers between devices, scatter_chunks(): buf = mine + lax.ppermute(other, axis, swap_pairs(axis, j))  67 us
    ppermute x7, waiting for transfers between devices, gather_chunks(): recv = lax.ppermute(buf, axis, swap_pairs(axis, j))  35.8 us
    ppermute x7, starting transfers between devices, gather_chunks(): recv = lax.ppermute(buf, axis, swap_pairs(axis, j))  18.1 us
    ppermute x7, starting transfers between devices, scatter_chunks(): buf = mine + lax.ppermute(other, axis, swap_pairs(axis, j))  13.2 us
    ppermute x2, waiting for transfers between devices, extended_2(): lax.ppermute(lax.slice_in_dim(block, 0, width, axis=dim), axis, backward)  8.4 us
    ppermute x2, waiting for transfers between devices, passed_along(): return lax.ppermute(array, axis, pairs)  8.25 us
    ppermute x2, starting transfers between devices, extended_2(): lax.ppermute(lax.slice_in_dim(block, block.shape[dim] - width, None, axis...  7.77 us
    reduce_sum x1, other arithmetic, pool_branch(): grad_part = jnp.sum(sent_mid.astype(jnp.float32) * act, axis=(0, 1))  7.22 us
  transfers between devices with their start and end apart: 24, of which 20 were waited for; matrix products, arithmetic and copies ran while one was open for 2% of the time, Pallas kernels for 0%

profile of v1, /device:TPU:1, one launch (start us, length us, event | category | flops | bytes accessed | tf_op | source)
XLA Modules:
  0.0 239.9 jit_solution(3920106451188080176)
XLA Ops:
  1.6 7.8 %collective-permute-start = (bf16[16,507]{1,0:T(8,128)(2,1)S(1)}, bf16[16,507]{1,0:T(8,128)(2,1)S(1)}, u32[]{:S(2)}, u32[]{:S(2)}) collective-permute-start(bf16[16,507]{1,0:T(8,128)(2,1)S(1)} %reshape_squeeze.9), channel_id=1, source_target_pairs={{0,32},{8,40},{16,48},{24,56},{32,0},{40,8},{48,16},{56,24},{64,96... | collective-permute-start | bytes 48680 | tf_op jit(solution)/shard_map/ppermute | solution.py:41
  10.6 2.8 %collective-permute-start.1 = (bf16[2,16,507]{2,1,0:T(8,128)(2,1)S(1)}, bf16[2,16,507]{2,1,0:T(8,128)(2,1)S(1)}, u32[]{:S(2)}, u32[]{:S(2)}) collective-permute-start(bf16[2,16,507]{2,1,0:T(8,128)(2,1)S(1)} %pad_maximum_fusion.7), channel_id=1, source_target_pairs={{0,128},{8,136},{16,144},{24,152},{32,160},{40,168},{48,176},{56,1... | collective-permute-start | bytes 97352 | tf_op jit(solution)/shard_map/ppermute | solution.py:41
  13.4 1.5 collective-permute-done.1
  15.0 1.5 collective-permute-start.2
  16.5 3.3 %collective-permute-done.2 = bf16[2,2,16,507]{3,2,1,0:T(8,128)(2,1)S(1)} collective-permute-done((bf16[2,2,16,507]{3,2,1,0:T(8,128)(2,1)S(1)}, bf16[2,2,16,507]{3,2,1,0:T(8,128)(2,1)S(1)}, u32[]{:S(2)}, u32[]{:S(2)}) %collective-permute-start.2) | collective-permute-done | bytes 64928 | tf_op jit(solution)/shard_map/ppermute | solution.py:41
  19.8 3.0 %collective-permute-start.3 = (bf16[2,2,2,16,507]{4,3,0,2,1:T(8,128)(2,1)S(1)}, bf16[2,2,2,16,507]{4,3,0,2,1:T(8,128)(2,1)S(1)}, u32[]{:S(2)}, u32[]{:S(2)}) collective-permute-start(bf16[2,2,2,16,507]{4,3,0,2,1:T(8,128)(2,1)S(1)} %pad_maximum_fusion.5), channel_id=1, source_target_pairs={{0,2},{1,3},{2,0},{3,1},{4,6},{5,7},{6,4},{7,5},{8,10},{9,11},{10,... | collective-permute-start | bytes 389384 | tf_op jit(solution)/shard_map/ppermute | solution.py:41
  22.8 2.4 %collective-permute-done.3 = bf16[2,2,2,16,507]{4,3,0,2,1:T(8,128)(2,1)S(1)} collective-permute-done((bf16[2,2,2,16,507]{4,3,0,2,1:T(8,128)(2,1)S(1)}, bf16[2,2,2,16,507]{4,3,0,2,1:T(8,128)(2,1)S(1)}, u32[]{:S(2)}, u32[]{:S(2)}) %collective-permute-start.3) | collective-permute-done | bytes 129824 | tf_op jit(solution)/shard_map/ppermute | solution.py:41
  26.6 4.0 %collective-permute-done.4 = bf16[2,2,2,2,16,507]{5,4,0,1,3,2:T(8,128)(2,1)S(1)} collective-permute-done((bf16[2,2,2,2,16,507]{5,4,0,1,3,2:T(8,128)(2,1)S(1)}, bf16[2,2,2,2,16,507]{5,4,0,1,3,2:T(8,128)(2,1)S(1)}, u32[]{:S(2)}, u32[]{:S(2)}) %collective-permute-start.4) | collective-permute-done | bytes 259616 | tf_op jit(solution)/shard_map/ppermute | solution.py:41
  30.9 7.9 %collective-permute-done.5 = bf16[2,2,2,2,2,16,507]{6,5,1,2,4,0,3:T(8,128)(2,1)S(1)} collective-permute-done((bf16[2,2,2,2,2,16,507]{6,5,1,2,4,0,3:T(8,128)(2,1)S(1)}, bf16[2,2,2,2,2,16,507]{6,5,1,2,4,0,3:T(8,128)(2,1)S(1)}, u32[]{:S(2)}, u32[]{:S(2)}) %collective-permute-start.5) | collective-permute-done | bytes 519200 | tf_op jit(solution)/shard_map/ppermute | solution.py:41
  39.0 1.4 collective-permute-start.6
  40.4 15.6 %collective-permute-done.6 = bf16[2,2,2,2,2,2,16,507]{7,6,2,0,3,5,1,4:T(8,128)(2,1)S(1)} collective-permute-done((bf16[2,2,2,2,2,2,16,507]{7,6,2,0,3,5,1,4:T(8,128)(2,1)S(1)}, bf16[2,2,2,2,2,2,16,507]{7,6,2,0,3,5,1,4:T(8,128)(2,1)S(1)}, u32[]{:S(2)}, u32[]{:S(2)}) %collective-permute-start.6) | collective-permute-done | bytes 1038368 | tf_op jit(solution)/shard_map/ppermute | solution.py:41
  56.2 1.6 maximum_bitcast_fusion
  57.8 5.3 %reshape_reshape.6 = bf16[416,2496]{1,0:T(8,128)(2,1)S(1)} reshape(bf16[2,2,2,2,2,2,2,16,507]{8,7,6,5,4,3,2,1,0:T(8,128)(2,1)} %maximum_bitcast_fusion) | data formatting | bytes 4153344 | tf_op jit(solution)/shard_map/reshape;reshape | solution.py:139
  63.1 3.6 %conditional.4 = (bf16[4,32,416]{2,1,0:T(8,128)(2,1)}, bf16[4,32,2496]{2,1,0:T(8,128)(2,1)S(1)}, f32[416,2496]{1,0:T(8,128)}) conditional(s32[]{:T(128)} %convert_element_type.231, bf16[4,32,2496]{2,1,0:T(8,128)(2,1)S(1)} %bitcast.127, (bf16[1,4,32,384]{3,2,1,0:T(8,128)(2,1)}, bf16[1,2,16,384]{3,2,1,0:T(8,128)(2,1)S(1)}, ...), branch_computations={%region_0.1_spmd, %region_1.2_spmd} | conditional | flops 573085696 | bytes 10971160 | solution.py:173
  63.5 2.5 %broadcast.58 = f32[416,2496]{1,0:T(8,128)} broadcast(f32[]{:T(128)} %constant.91.clone), dimensions={} | broadcast | bytes 4153348 | tf_op jit(solution)/shard_map/broadcast.4
  67.6 4.4 %collective-permute-start.8 = (bf16[2,32,2496]{2,1,0:T(8,128)(2,1)}, bf16[2,32,2496]{2,1,0:T(8,128)(2,1)}, u32[]{:S(2)}, u32[]{:S(2)}) collective-permute-start(bf16[2,32,2496]{2,1,0:T(8,128)(2,1)} %get-tuple-element.181), channel_id=1, source_target_pairs={{0,1},{1,2},{2,3},{4,5},{5,6},{6,7},{8,9},{9,10},{10,11},{12,13},{... | collective-permute-start | bytes 958472 | tf_op jit(solution)/shard_map/ppermute | solution.py:12
  74.6 1.7 convert_element_type.232
  76.2 3.9 %collective-permute-done.9 = bf16[2,32,2496]{2,1,0:T(8,128)(2,1)} collective-permute-done((bf16[2,32,2496]{2,1,0:T(8,128)(2,1)}, bf16[2,32,2496]{2,1,0:T(8,128)(2,1)}, u32[]{:S(2)}, u32[]{:S(2)}) %collective-permute-start.9) | collective-permute-done | bytes 319520 | tf_op jit(solution)/shard_map/ppermute | solution.py:15
  81.3 8.3 %collective-permute-done.7 = bf16[4,32,2496]{2,1,0:T(8,128)(2,1)} collective-permute-done((bf16[4,32,2496]{2,1,0:T(8,128)(2,1)S(1)}, bf16[4,32,2496]{2,1,0:T(8,128)(2,1)}, u32[]{:S(2)}, u32[]{:S(2)}) %collective-permute-start.7) | collective-permute-done | bytes 639008 | tf_op jit(solution)/shard_map/ppermute | solution.py:23
  89.6 7.9 %conditional.5 = (f32[4,32,2496]{2,1,0:T(8,128)}, f32[2496]{0:T(1024)S(1)}, f32[2496]{0:T(1024)S(1)}) conditional(s32[]{:T(128)} %convert_element_type.230, () %tuple.43, (f32[25,2496]{1,0:T(8,128)S(1)}, bf16[8,32,2496]{2,1,0:T(8,128)(2,1)S(1)}, bf16[4,32,2496]{2,1,0:T(8,128)(2,1)}) %tuple.119), branch_computations={%region_2.3_spmd, %region_3.6_spmd} | conditional | flops 26193024 | bytes 7330840 | solution.py:191
  90.3 7.2 %multiply_reduce_fusion = (f32[2496]{0:T(1024)S(1)}, f32[2496]{0:T(1024)S(1)}, f32[4,32,2496]{2,1,0:T(8,128)}) fusion(bf16[4,32,2496]{2,1,0:T(8,128)(2,1)} %get-tuple-element.71, f32[2496]{0:T(1024)S(1)} %get-tuple-element.121, f32[2496]{0:T(1024)S(1)} %get-tuple-element.122, bf16[8,32,2496]{2,1,0:T(8,128)(2,1)S(1)} %get-tuple-element.70, ...), kind=kLoop, calls=%fused_computation.13 | loop fusion | flops 26193024 | bytes 6831616 | tf_op jit(solution)/shard_map/cond/branch_1_fun/reduce_sum | solution.py:181
  97.5 2.4 collective-permute-start.12
  99.9 1.4 collective-permute-done.12
  101.3 2.3 collective-permute-start.13
  103.6 1.5 collective-permute-start.11
  105.0 1.4 copy.38
  107.7 5.7 %conditional.6 = (bf16[4,32,2496]{2,1,0:T(8,128)(2,1)S(1)}) conditional(s32[]{:T(128)} %convert_element_type.230, () %tuple.42, (bf16[4,32,2496]{2,1,0:T(8,128)(2,1)}, f32[2496]{0:T(1024)S(1)}, f32[2496]{0:T(1024)S(1)}, f32[2496,104]{1,0:T(8,128)S(1)}, f32[104,2496]{1,0:T(8,128)S(1)}, /*index=5*/f32[2496]{0:T(1024)S(1)}, f32[2496]{0:T(1024)S(1)}, ...), branch_computations={%region_6.7_spmd, %region_7.8_spmd} | conditional | flops 16320096 | bytes 6911016 | solution.py:203
  111.4 2.0 multiply_convert_fusion
  114.3 3.4 %collective-permute-start.14 = (bf16[2,32,2496]{2,1,0:T(8,128)(2,1)}, bf16[2,32,2496]{2,1,0:T(8,128)(2,1)}, u32[]{:S(2)}, u32[]{:S(2)}) collective-permute-start(bf16[2,32,2496]{2,1,0:T(8,128)(2,1)} %get-tuple-element.179), channel_id=1, source_target_pairs={{0,1},{1,2},{2,3},{4,5},{5,6},{6,7},{8,9},{9,10},{10,11},{12,13},{... | collective-permute-start | bytes 958472 | tf_op jit(solution)/shard_map/ppermute | solution.py:12
  121.3 4.5 %collective-permute-done.15 = bf16[2,32,2496]{2,1,0:T(8,128)(2,1)} collective-permute-done((bf16[2,32,2496]{2,1,0:T(8,128)(2,1)}, bf16[2,32,2496]{2,1,0:T(8,128)(2,1)}, u32[]{:S(2)}, u32[]{:S(2)}) %collective-permute-start.15) | collective-permute-done | bytes 319520 | tf_op jit(solution)/shard_map/ppermute | solution.py:15
  127.1 11.0 %conditional.7 = (f32[416,2496]{1,0:T(8,128)}, bf16[1,1,4,32,416]{4,3,2,1,0:T(8,128)(2,1)}) conditional(s32[]{:T(128)} %convert_element_type.230, (bf16[4,32,416]{2,1,0:T(8,128)(2,1)}, f32[416,2496]{1,0:T(8,128)}) %tuple.114, (f32[25,2496]{1,0:T(8,128)S(1)}, bf16[8,32,2496]{2,1,0:T(8,128)(2,1)S(1)}, bf16[4,32,2496]{2,1,0:T(8,128)(2,1)S(1)}, ...), branch_computations={%region_8.9_spmd, %region_9.10_spmd} | conditional | flops 558624768 | bytes 15580688 | solution.py:223
  128.0 5.6 %fusion.24 = bf16[4,32,2496]{2,1,0:T(8,128)(2,1)S(1)} fusion(bf16[4,32,2496]{2,1,0:T(8,128)(2,1)S(1)} %get-tuple-element.84, bf16[8,32,2496]{2,1,0:T(8,128)(2,1)S(1)} %get-tuple-element.83, f32[2496]{0:T(1024)S(1)} %get-tuple-element.146, f32[2496]{0:T(1024)S(1)} %get-tuple-element.147, f32[2496]{0:T(1024)S(1)} %get-tuple-element.148, ...), kind=kLoop, calls=%fused_computation.88 | loop fusion | flops 26836992 | bytes 6189056 | tf_op jit(solution)/shard_map/cond/branch_1_fun/convert_element_type | solution.py:210
  133.6 2.8 %convolution_bitcast_fusion.2 = f32[416,2496]{1,0:T(8,128)} fusion(bf16[128,2496]{1,0:T(8,128)(2,1)S(1)} %bitcast.131, bf16[128,416]{1,0:T(8,128)(2,1)S(1)} %bitcast.134), kind=kOutput, calls=%fused_computation.79 | convolution fusion | flops 265814016 | bytes 4898816 | tf_op jit(solution)/shard_map/cond/branch_1_fun/dot_general | solution.py:213
  138.0 4.5 %broadcast_multiply_fusion.1 = f32[416,2496]{1,0:T(8,128)} fusion(f32[416,2496]{1,0:T(8,128)} %get-tuple-element.105), kind=kLoop, calls=%fused_computation.137 | loop fusion | flops 1038336 | bytes 8306688 | tf_op jit(solution)/shard_map/div | solution.py:225
  142.5 7.2 %reshape_reshape.7 = f32[2,2,2,2,2,2,2,8,1014]{8,7,6,5,4,3,2,1,0:T(8,128)} reshape(f32[416,2496]{1,0:T(8,128)} %broadcast_multiply_fusion.1) | data formatting | bytes 8306688 | tf_op jit(solution)/shard_map/reshape;reshape | solution.py:53
  149.6 2.7 %constant_dynamic-slice_fusion.1 = (f32[2,2,2,2,2,2,1,8,1014]{8,7,6,5,4,3,2,1,0:T(8,128)S(1)}, f32[2,2,2,2,2,2,1,8,1014]{8,7,6,5,4,3,2,1,0:T(8,128)S(1)}) fusion(f32[2,2,2,2,2,2,2,8,1014]{8,7,6,5,4,3,2,1,0:T(8,128)} %reshape_reshape.7, s32[]{:T(128)S(6)} %select_n.154, s32[]{:T(128)S(6)} %select_n.155), kind=kLoop, calls=%fused_computation.176 | loop fusion | bytes 8306696 | tf_op jit(solution)/shard_map/jit(dynamic_index_in_dim)/dynamic_slice | solution.py:58
  152.3 1.5 copy.43
  153.8 33.6 %collective-permute-done.17 = f32[2,2,2,2,2,2,8,1014]{7,6,5,3,2,0,1,4:T(8,128)} collective-permute-done((f32[2,2,2,2,2,2,8,1014]{7,6,5,3,2,0,1,4:T(8,128)}, f32[2,2,2,2,2,2,8,1014]{7,6,5,3,2,0,1,4:T(8,128)}, u32[]{:S(2)}, u32[]{:S(2)}) %collective-permute-start.17) | collective-permute-done | bytes 2076704 | tf_op jit(solution)/shard_map/ppermute | solution.py:60
  187.4 2.0 bitcast_add_fusion
  191.0 13.5 %collective-permute-done.18 = f32[2,2,2,2,2,8,1014]{6,5,4,3,2,0,1:T(8,128)S(1)} collective-permute-done((f32[2,2,2,2,2,8,1014]{6,5,4,3,2,0,1:T(8,128)S(1)}, f32[2,2,2,2,2,8,1014]{6,5,4,3,2,0,1:T(8,128)S(1)}, u32[]{:S(2)}, u32[]{:S(2)}) %collective-permute-start.18) | collective-permute-done | bytes 1038368 | tf_op jit(solution)/shard_map/ppermute | solution.py:60
  204.6 1.4 bitcast_add_fusion.1
  207.3 6.8 %collective-permute-done.19 = f32[2,2,2,2,8,1014]{5,4,3,2,1,0:T(8,128)S(1)} collective-permute-done((f32[2,2,2,2,8,1014]{5,4,3,2,1,0:T(8,128)S(1)}, f32[2,2,2,2,8,1014]{5,4,3,2,1,0:T(8,128)S(1)}, u32[]{:S(2)}, u32[]{:S(2)}) %collective-permute-start.19) | collective-permute-done | bytes 519200 | tf_op jit(solution)/shard_map/ppermute | solution.py:60
  214.3 2.2 collective-permute-start.20
  216.5 4.6 %collective-permute-done.20 = f32[2,2,2,8,1014]{4,3,2,1,0:T(8,128)S(1)} collective-permute-done((f32[2,2,2,8,1014]{4,3,2,1,0:T(8,128)S(1)}, f32[2,2,2,8,1014]{4,3,2,1,0:T(8,128)S(1)}, u32[]{:S(2)}, u32[]{:S(2)}) %collective-permute-start.20) | collective-permute-done | bytes 259616 | tf_op jit(solution)/shard_map/ppermute | solution.py:60
  222.4 4.9 %collective-permute-done.21 = f32[2,2,8,1014]{3,2,1,0:T(8,128)S(1)} collective-permute-done((f32[2,2,8,1014]{3,2,1,0:T(8,128)S(1)}, f32[2,2,8,1014]{3,2,1,0:T(8,128)S(1)}, u32[]{:S(2)}, u32[]{:S(2)}) %collective-permute-start.21) | collective-permute-done | bytes 129824 | tf_op jit(solution)/shard_map/ppermute | solution.py:60
  227.4 2.8 %collective-permute-start.22 = (f32[2,8,1014]{2,1,0:T(8,128)S(1)}, f32[2,8,1014]{2,1,0:T(8,128)S(1)}, u32[]{:S(2)}, u32[]{:S(2)}) collective-permute-start(f32[2,8,1014]{2,1,0:T(8,128)S(1)} %dynamic-slice_bitcast_fusion.4), channel_id=1, source_target_pairs={{0,128},{8,136},{16,144},{24,152},{32,160},{40,168},{48,176},{56,1... | collective-permute-start | bytes 194696 | tf_op jit(solution)/shard_map/ppermute | solution.py:60
  230.2 2.2 collective-permute-done.22
  232.4 5.4 %collective-permute-start.23 = (f32[8,1014]{1,0:T(8,128)S(1)}, f32[8,1014]{1,0:T(8,128)S(1)}, u32[]{:S(2)}, u32[]{:S(2)}) collective-permute-start(f32[8,1014]{1,0:T(8,128)S(1)} %dynamic-slice_bitcast_fusion.5), channel_id=1, source_target_pairs={{0,32},{8,40},{16,48},{24,56},{32,0},{40,8},{48,16},{56,24},{64,96... | collective-permute-start | bytes 97352 | tf_op jit(solution)/shard_map/ppermute | solution.py:60
  (89 shorter events, 30.0 us)
Async XLA Ops:
  1.6 9.0 %collective-permute-start = (bf16[16,507]{1,0:T(8,128)(2,1)S(1)}, bf16[16,507]{1,0:T(8,128)(2,1)S(1)}, u32[]{:S(2)}, u32[]{:S(2)}) collective-permute-start(bf16[16,507]{1,0:T(8,128)(2,1)S(1)} %reshape_squeeze.9), channel_id=1, source_target_pairs={{0,32},{8,40},{16,48},{24,56},{32,0},{40,8},{48,16},{56,24},{64,96... | collective-permute-start | bytes 48680 | tf_op jit(solution)/shard_map/ppermute | solution.py:41
  10.6 4.4 %collective-permute-start.1 = (bf16[2,16,507]{2,1,0:T(8,128)(2,1)S(1)}, bf16[2,16,507]{2,1,0:T(8,128)(2,1)S(1)}, u32[]{:S(2)}, u32[]{:S(2)}) collective-permute-start(bf16[2,16,507]{2,1,0:T(8,128)(2,1)S(1)} %pad_maximum_fusion.7), channel_id=1, source_target_pairs={{0,128},{8,136},{16,144},{24,152},{32,160},{40,168},{48,176},{56,1... | collective-permute-start | bytes 97352 | tf_op jit(solution)/shard_map/ppermute | solution.py:41
  15.0 4.8 %collective-permute-start.2 = (bf16[2,2,16,507]{3,2,1,0:T(8,128)(2,1)S(1)}, bf16[2,2,16,507]{3,2,1,0:T(8,128)(2,1)S(1)}, u32[]{:S(2)}, u32[]{:S(2)}) collective-permute-start(bf16[2,2,16,507]{3,2,1,0:T(8,128)(2,1)S(1)} %pad_maximum_fusion.6), channel_id=1, source_target_pairs={{0,16},{8,24},{16,0},{24,8},{32,48},{40,56},{48,32},{56,40},{64,80... | collective-permute-start | bytes 194696 | tf_op jit(solution)/shard_map/ppermute | solution.py:41
  19.8 5.4 %collective-permute-start.3 = (bf16[2,2,2,16,507]{4,3,0,2,1:T(8,128)(2,1)S(1)}, bf16[2,2,2,16,507]{4,3,0,2,1:T(8,128)(2,1)S(1)}, u32[]{:S(2)}, u32[]{:S(2)}) collective-permute-start(bf16[2,2,2,16,507]{4,3,0,2,1:T(8,128)(2,1)S(1)} %pad_maximum_fusion.5), channel_id=1, source_target_pairs={{0,2},{1,3},{2,0},{3,1},{4,6},{5,7},{6,4},{7,5},{8,10},{9,11},{10,... | collective-permute-start | bytes 389384 | tf_op jit(solution)/shard_map/ppermute | solution.py:41
  25.3 5.3 %collective-permute-start.4 = (bf16[2,2,2,2,16,507]{5,4,0,1,3,2:T(8,128)(2,1)S(1)}, bf16[2,2,2,2,16,507]{5,4,0,1,3,2:T(8,128)(2,1)S(1)}, u32[]{:S(2)}, u32[]{:S(2)}) collective-permute-start(bf16[2,2,2,2,16,507]{5,4,0,1,3,2:T(8,128)(2,1)S(1)} %pad_maximum_fusion.4), channel_id=1, source_target_pairs={{0,64},{8,72},{16,80},{24,88},{32,96},{40,104},{48,112},{56,120},{... | collective-permute-start | bytes 778760 | tf_op jit(solution)/shard_map/ppermute | solution.py:41
  30.7 8.1 %collective-permute-start.5 = (bf16[2,2,2,2,2,16,507]{6,5,1,2,4,0,3:T(8,128)(2,1)S(1)}, bf16[2,2,2,2,2,16,507]{6,5,1,2,4,0,3:T(8,128)(2,1)S(1)}, u32[]{:S(2)}, u32[]{:S(2)}) collective-permute-start(bf16[2,2,2,2,2,16,507]{6,5,1,2,4,0,3:T(8,128)(2,1)S(1)} %pad_maximum_fusion.3), channel_id=1, source_target_pairs={{0,8},{8,0},{16,24},{24,16},{32,40},{40,32},{48,56},{56,48},{64,72... | collective-permute-start | bytes 1557512 | tf_op jit(solution)/shard_map/ppermute | solution.py:41
  39.0 17.0 %collective-permute-start.6 = (bf16[2,2,2,2,2,2,16,507]{7,6,2,0,3,5,1,4:T(8,128)(2,1)S(1)}, bf16[2,2,2,2,2,2,16,507]{7,6,2,0,3,5,1,4:T(8,128)(2,1)S(1)}, u32[]{:S(2)}, u32[]{:S(2)}) collective-permute-start(bf16[2,2,2,2,2,2,16,507]{7,6,2,0,3,5,1,4:T(8,128)(2,1)S(1)} %pad_maximum_fusion.2), channel_id=1, source_target_pairs={{0,1},{1,0},{2,3},{3,2},{4,5},{5,4},{6,7},{7,6},{8,9},{9,8},{10,11... | collective-permute-start | bytes 3115016 | tf_op jit(solution)/shard_map/ppermute | solution.py:41
  57.8 5.3 %copy-start.1 = (bf16[1,1,4,32,2496]{4,3,2,1,0:T(8,128)(2,1)S(1)}, bf16[1,1,4,32,2496]{4,3,2,1,0:T(8,128)(2,1)}, u32[]{:S(2)}) copy-start(bf16[1,1,4,32,2496]{4,3,2,1,0:T(8,128)(2,1)} %param.19) | copy-start | bytes 1916932
  57.8 5.3 %copy-start.6 = (bf16[1,2,16,384]{3,2,1,0:T(8,128)(2,1)S(1)}, bf16[1,2,16,384]{3,2,1,0:T(8,128)(2,1)}, u32[]{:S(2)}) copy-start(bf16[1,2,16,384]{3,2,1,0:T(8,128)(2,1)} %param.21) | copy-start | bytes 73732
  57.8 5.3 %copy-start.7 = (bf16[1,1,8,384]{3,2,1,0:T(8,128)(2,1)S(1)}, bf16[1,1,8,384]{3,2,1,0:T(8,128)(2,1)}, u32[]{:S(2)}) copy-start(bf16[1,1,8,384]{3,2,1,0:T(8,128)(2,1)} %param.22) | copy-start | bytes 18436
  67.6 8.7 %collective-permute-start.8 = (bf16[2,32,2496]{2,1,0:T(8,128)(2,1)}, bf16[2,32,2496]{2,1,0:T(8,128)(2,1)}, u32[]{:S(2)}, u32[]{:S(2)}) collective-permute-start(bf16[2,32,2496]{2,1,0:T(8,128)(2,1)} %get-tuple-element.181), channel_id=1, source_target_pairs={{0,1},{1,2},{2,3},{4,5},{5,6},{6,7},{8,9},{9,10},{10,11},{12,13},{... | collective-permute-start | bytes 958472 | tf_op jit(solution)/shard_map/ppermute | solution.py:12
  72.0 8.1 %collective-permute-start.9 = (bf16[2,32,2496]{2,1,0:T(8,128)(2,1)}, bf16[2,32,2496]{2,1,0:T(8,128)(2,1)}, u32[]{:S(2)}, u32[]{:S(2)}) collective-permute-start(bf16[2,32,2496]{2,1,0:T(8,128)(2,1)} %get-tuple-element.182), channel_id=1, source_target_pairs={{1,0},{2,1},{3,2},{5,4},{6,5},{7,6},{9,8},{10,9},{11,10},{13,12},{... | collective-permute-start | bytes 958472 | tf_op jit(solution)/shard_map/ppermute | solution.py:15
  73.3 16.3 %collective-permute-start.7 = (bf16[4,32,2496]{2,1,0:T(8,128)(2,1)S(1)}, bf16[4,32,2496]{2,1,0:T(8,128)(2,1)}, u32[]{:S(2)}, u32[]{:S(2)}) collective-permute-start(bf16[4,32,2496]{2,1,0:T(8,128)(2,1)S(1)} %get-tuple-element.100), channel_id=1, source_target_pairs={{0,4},{1,5},{2,6},{3,7},{8,12},{9,13},{10,14},{11,15},{16,20},{17,... | collective-permute-start | bytes 1916936 | tf_op jit(solution)/shard_map/ppermute | solution.py:23
  76.2 13.3 %copy-start.2 = (f32[25,2496]{1,0:T(8,128)S(1)}, f32[25,2496]{1,0:T(8,128)}, u32[]{:S(2)}) copy-start(f32[25,2496]{1,0:T(8,128)} %convert_element_type.232) | copy-start | bytes 748804
  97.5 3.8 %collective-permute-start.12 = (f32[2496]{0:T(1024)S(1)}, f32[2496]{0:T(1024)S(1)}, u32[]{:S(2)}, u32[]{:S(2)}) collective-permute-start(f32[2496]{0:T(1024)S(1)} %get-tuple-element.102), channel_id=1, source_target_pairs={{0,1},{1,0},{2,3},{3,2},{4,5},{5,4},{6,7},{7,6},{8,9},{9,8},{10,11... | collective-permute-start | bytes 29960 | tf_op jit(solution)/shard_map/ppermute | solution.py:67
  99.9 3.7 %collective-permute-start.10 = (f32[2496]{0:T(1024)S(1)}, f32[2496]{0:T(1024)S(1)}, u32[]{:S(2)}, u32[]{:S(2)}) collective-permute-start(f32[2496]{0:T(1024)S(1)} %get-tuple-element.101), channel_id=1, source_target_pairs={{0,1},{1,0},{2,3},{3,2},{4,5},{5,4},{6,7},{7,6},{8,9},{9,8},{10,11... | collective-permute-start | bytes 29960 | tf_op jit(solution)/shard_map/ppermute | solution.py:67
  101.3 6.3 %collective-permute-start.13 = (f32[2496]{0:T(1024)S(1)}, f32[2496]{0:T(1024)S(1)}, u32[]{:S(2)}, u32[]{:S(2)}) collective-permute-start(f32[2496]{0:T(1024)S(1)} %add.288), channel_id=1, source_target_pairs={{0,2},{1,3},{2,0},{3,1},{4,6},{5,7},{6,4},{7,5},{8,10},{9,11},{10,... | collective-permute-start | bytes 29960 | tf_op jit(solution)/shard_map/ppermute | solution.py:67
  103.6 4.2 %collective-permute-start.11 = (f32[2496]{0:T(1024)S(1)}, f32[2496]{0:T(1024)S(1)}, u32[]{:S(2)}, u32[]{:S(2)}) collective-permute-start(f32[2496]{0:T(1024)S(1)} %add.287), channel_id=1, source_target_pairs={{0,2},{1,3},{2,0},{3,1},{4,6},{5,7},{6,4},{7,5},{8,10},{9,11},{10,... | collective-permute-start | bytes 29960 | tf_op jit(solution)/shard_map/ppermute | solution.py:67
  106.4 1.1 copy-start.4
  114.3 7.0 %collective-permute-start.14 = (bf16[2,32,2496]{2,1,0:T(8,128)(2,1)}, bf16[2,32,2496]{2,1,0:T(8,128)(2,1)}, u32[]{:S(2)}, u32[]{:S(2)}) collective-permute-start(bf16[2,32,2496]{2,1,0:T(8,128)(2,1)} %get-tuple-element.179), channel_id=1, source_target_pairs={{0,1},{1,2},{2,3},{4,5},{5,6},{6,7},{8,9},{9,10},{10,11},{12,13},{... | collective-permute-start | bytes 958472 | tf_op jit(solution)/shard_map/ppermute | solution.py:12
  117.7 8.1 %collective-permute-start.15 = (bf16[2,32,2496]{2,1,0:T(8,128)(2,1)}, bf16[2,32,2496]{2,1,0:T(8,128)(2,1)}, u32[]{:S(2)}, u32[]{:S(2)}) collective-permute-start(bf16[2,32,2496]{2,1,0:T(8,128)(2,1)} %get-tuple-element.180), channel_id=1, source_target_pairs={{1,0},{2,1},{3,2},{5,4},{6,5},{7,6},{9,8},{10,9},{11,10},{13,12},{... | collective-permute-start | bytes 958472 | tf_op jit(solution)/shard_map/ppermute | solution.py:15
  119.0 8.1 %collective-permute-start.16 = (bf16[4,32,416]{2,1,0:T(8,128)(2,1)}, bf16[4,32,416]{2,1,0:T(8,128)(2,1)S(1)}, u32[]{:S(2)}, u32[]{:S(2)}) collective-permute-start(bf16[4,32,416]{2,1,0:T(8,128)(2,1)} %get-tuple-element.209), channel_id=1, source_target_pairs={{0,4},{1,5},{2,6},{3,7},{8,12},{9,13},{10,14},{11,15},{16,20},{17,... | collective-permute-start | bytes 319496 | tf_op jit(solution)/shard_map/ppermute | solution.py:23
  120.3 6.8 %copy-start.3 = (f32[25,2496]{1,0:T(8,128)S(1)}, f32[25,2496]{1,0:T(8,128)}, u32[]{:S(2)}) copy-start(f32[25,2496]{1,0:T(8,128)} %convert_element_type.232) | copy-start | bytes 748804
  120.3 6.8 %copy-start.5 = (bf16[1,4,32,416]{3,2,1,0:T(8,128)(2,1)S(1)}, bf16[1,4,32,416]{3,2,1,0:T(8,128)(2,1)}, u32[]{:S(2)}) copy-start(bf16[1,4,32,416]{3,2,1,0:T(8,128)(2,1)} %param.18) | copy-start | bytes 319492
  153.8 33.6 %collective-permute-start.17 = (f32[2,2,2,2,2,2,8,1014]{7,6,5,3,2,0,1,4:T(8,128)}, f32[2,2,2,2,2,2,8,1014]{7,6,5,3,2,0,1,4:T(8,128)}, u32[]{:S(2)}, u32[]{:S(2)}) collective-permute-start(f32[2,2,2,2,2,2,8,1014]{7,6,5,3,2,0,1,4:T(8,128)} %bitcast.126), channel_id=1, source_target_pairs={{0,1},{1,0},{2,3},{3,2},{4,5},{5,4},{6,7},{7,6},{8,9},{9,8},{10,11... | collective-permute-start | bytes 6230024 | tf_op jit(solution)/shard_map/ppermute | solution.py:60
  189.4 1.4 copy-start
  190.8 13.7 %collective-permute-start.18 = (f32[2,2,2,2,2,8,1014]{6,5,4,3,2,0,1:T(8,128)S(1)}, f32[2,2,2,2,2,8,1014]{6,5,4,3,2,0,1:T(8,128)S(1)}, u32[]{:S(2)}, u32[]{:S(2)}) collective-permute-start(f32[2,2,2,2,2,8,1014]{6,5,4,3,2,0,1:T(8,128)S(1)} %dynamic-slice_bitcast_fusion), channel_id=1, source_target_pairs={{0,8},{8,0},{16,24},{24,16},{32,40},{40,32},{48,56},{56,48},{64,72... | collective-permute-start | bytes 3115016 | tf_op jit(solution)/shard_map/ppermute | solution.py:60
  206.0 8.1 %collective-permute-start.19 = (f32[2,2,2,2,8,1014]{5,4,3,2,1,0:T(8,128)S(1)}, f32[2,2,2,2,8,1014]{5,4,3,2,1,0:T(8,128)S(1)}, u32[]{:S(2)}, u32[]{:S(2)}) collective-permute-start(f32[2,2,2,2,8,1014]{5,4,3,2,1,0:T(8,128)S(1)} %dynamic-slice_bitcast_fusion.1), channel_id=1, source_target_pairs={{0,64},{8,72},{16,80},{24,88},{32,96},{40,104},{48,112},{56,120},{... | collective-permute-start | bytes 1557512 | tf_op jit(solution)/shard_map/ppermute | solution.py:60
  214.3 6.8 %collective-permute-start.20 = (f32[2,2,2,8,1014]{4,3,2,1,0:T(8,128)S(1)}, f32[2,2,2,8,1014]{4,3,2,1,0:T(8,128)S(1)}, u32[]{:S(2)}, u32[]{:S(2)}) collective-permute-start(f32[2,2,2,8,1014]{4,3,2,1,0:T(8,128)S(1)} %dynamic-slice_bitcast_fusion.2), channel_id=1, source_target_pairs={{0,2},{1,3},{2,0},{3,1},{4,6},{5,7},{6,4},{7,5},{8,10},{9,11},{10,... | collective-permute-start | bytes 778760 | tf_op jit(solution)/shard_map/ppermute | solution.py:60
  221.1 6.2 %collective-permute-start.21 = (f32[2,2,8,1014]{3,2,1,0:T(8,128)S(1)}, f32[2,2,8,1014]{3,2,1,0:T(8,128)S(1)}, u32[]{:S(2)}, u32[]{:S(2)}) collective-permute-start(f32[2,2,8,1014]{3,2,1,0:T(8,128)S(1)} %dynamic-slice_bitcast_fusion.3), channel_id=1, source_target_pairs={{0,16},{8,24},{16,0},{24,8},{32,48},{40,56},{48,32},{56,40},{64,80... | collective-permute-start | bytes 389384 | tf_op jit(solution)/shard_map/ppermute | solution.py:60
  227.4 5.0 %collective-permute-start.22 = (f32[2,8,1014]{2,1,0:T(8,128)S(1)}, f32[2,8,1014]{2,1,0:T(8,128)S(1)}, u32[]{:S(2)}, u32[]{:S(2)}) collective-permute-start(f32[2,8,1014]{2,1,0:T(8,128)S(1)} %dynamic-slice_bitcast_fusion.4), channel_id=1, source_target_pairs={{0,128},{8,136},{16,144},{24,152},{32,160},{40,168},{48,176},{56,1... | collective-permute-start | bytes 194696 | tf_op jit(solution)/shard_map/ppermute | solution.py:60
  232.4 6.8 %collective-permute-start.23 = (f32[8,1014]{1,0:T(8,128)S(1)}, f32[8,1014]{1,0:T(8,128)S(1)}, u32[]{:S(2)}, u32[]{:S(2)}) collective-permute-start(f32[8,1014]{1,0:T(8,128)S(1)} %dynamic-slice_bitcast_fusion.5), channel_id=1, source_target_pairs={{0,32},{8,40},{16,48},{24,56},{32,0},{40,8},{48,16},{56,24},{64,96... | collective-permute-start | bytes 97352 | tf_op jit(solution)/shard_map/ppermute | solution.py:60
